TPU v7x, 512 devices: a whole 4x8x8 slice. The times are simulated.
512 devices in a mesh: dp: 16 (over y, core), tensor: 32 (over z, x).
Axes of the slice: x: 4, y: 8, z: 8, core: 2. Of those that a mesh axis runs over, the one named last changes fastest.
Arguments:
- layer_input: bfloat16 [65536, 8192], P('dp', 'tensor'), may hold values from -6 to 6
- output_grad: bfloat16 [65536, 1024], P(('dp', 'tensor')), may hold values from -6 to 6
- key_weight: bfloat16 [8192, 1024], P('tensor'), may hold values from -0.0625 to 0.0625
- adapter_down: bfloat16 [128, 16, 8192], P('dp', None, 'tensor'), may hold values from -0.0625 to 0.0625
- adapter_up: bfloat16 [128, 16, 1024], P('dp', None, 'tensor'), may hold values from -0.1875 to 0.1875
- segment_adapter: int32 [512], replicated, may hold values from 0 to 127
- adapter_slot: int32 [128], replicated, may hold values from 0 to 127, each once
- live_segments: int32 [16], P('dp'), may hold values from 1 to 32, as said below
Outputs:
- input_grad: bfloat16 [65536, 8192], P('dp', 'tensor')
- down_grad: bfloat16 [128, 16, 8192], P('dp', None, 'tensor')
- up_grad: bfloat16 [128, 16, 1024], P('dp', None, 'tensor')
Inputs may be any that keep to these rules, and one draw needn't show every extreme that they name: `live_segments`: some data group has all 32 segments live; a group's segments at or past its count are padding.
All inputs are finite; a program needn't handle non-finite values.
Results may differ from a plain program's by a relative error of at most 0.0057.
Values may be sent and summed in bfloat16 or wider, within the bound.
No kernel may reach another device: no remote copies, remote signals or barrier semaphores. Data moves between devices by JAX's collectives and lax.ppermute only.
A program may use at most 64 MiB of HBM per device.

v0:
```python
import jax
import jax.numpy as jnp
from jax import lax
from jax.sharding import PartitionSpec as P


def on_device(
    layer_input,
    output_grad,
    key_weight,
    adapter_down,
    adapter_up,
    segment_adapter,
    adapter_slot,
    live_segments,
):
    tensor_size = lax.axis_size("tensor")
    position = lax.axis_index("tensor")
    group_count = lax.axis_size("dp")
    group_index = lax.axis_index("dp")
    row_count = output_grad.shape[0]
    tok_group = layer_input.shape[0]
    width_shard = layer_input.shape[1]
    key_width = output_grad.shape[1]
    key_shard = key_width // tensor_size
    adapters = adapter_slot.shape[0]
    rank_dim = adapter_down.shape[1]
    per_owner = adapter_down.shape[0]
    seg_total = segment_adapter.shape[0]
    seg_group = seg_total // group_count
    seg_len = tok_group // seg_group
    f32 = jnp.float32
    bf16 = jnp.bfloat16
    whole_raw = lax.all_gather(output_grad, "tensor", axis=0, tiled=True)
    slot_ids = jnp.arange(adapters, dtype=jnp.int32)
    lookup = segment_adapter[:, None] == slot_ids[None, :]
    every_slot = jnp.sum(jnp.where(lookup, adapter_slot[None, :], 0), axis=1)
    seg_slot = lax.dynamic_slice_in_dim(every_slot, group_index * seg_group, seg_group)
    seg_live = jnp.arange(seg_group, dtype=jnp.int32) < live_segments[0]
    local_store = jnp.concatenate([adapter_down, adapter_up], axis=2).reshape(per_owner, -1)
    spread = jnp.broadcast_to(local_store[None], (group_count,) + local_store.shape)
    stores = lax.all_to_all(spread, "dp", 0, 0, tiled=True).reshape(adapters, -1)
    choose = (seg_slot[:, None] == slot_ids[None, :]).astype(bf16)
    seg_store = jnp.dot(choose, stores, preferred_element_type=f32).astype(bf16)
    seg_store = seg_store.reshape(seg_group, rank_dim, width_shard + key_shard)
    down_seg = seg_store[:, :, :width_shard]
    up_seg = seg_store[:, :, width_shard:]
    input_seg = layer_input.reshape(seg_group, seg_len, width_shard)
    proj_part = jnp.einsum("sjd,srd->srj", input_seg, down_seg, preferred_element_type=f32)
    first = jnp.concatenate([proj_part, up_seg.astype(f32)], axis=2).reshape(seg_group, -1)
    first = lax.all_to_all(first, "tensor", 0, 0, tiled=True)
    first = first.reshape(tensor_size, rank_dim, seg_len + key_shard)
    projected_own = jnp.sum(first[:, :, :seg_len], axis=0).astype(bf16)
    up_own = jnp.transpose(first[:, :, seg_len:], (1, 0, 2)).reshape(rank_dim, key_width)
    up_own = up_own.astype(bf16)
    own_live = position < live_segments[0]
    masked_own = jnp.where(own_live, output_grad, jnp.zeros_like(output_grad))
    lowrank_own = lax.dot_general(
        up_own, masked_own, (((1,), (1,)), ((), ())), preferred_element_type=f32
    ).astype(bf16)
    seg_up_own = 2.0 * jnp.dot(projected_own, masked_own, preferred_element_type=f32)
    low_spread = jnp.broadcast_to(
        lowrank_own.reshape(1, row_count * rank_dim), (tensor_size, row_count * rank_dim)
    )
    up_pieces = jnp.transpose(
        seg_up_own.reshape(rank_dim, tensor_size, key_shard), (1, 0, 2)
    ).reshape(tensor_size, rank_dim * key_shard)
    up_round = lax.reduce_precision(up_pieces, exponent_bits=8, mantissa_bits=7)
    up_high = up_round.astype(bf16)
    up_low = (up_pieces - up_round).astype(bf16)
    second = jnp.concatenate([low_spread, up_high, up_low], axis=1)
    second = second.reshape(tensor_size, -1, 128)
    second = lax.all_to_all(second, "tensor", 0, 0, tiled=True).reshape(tensor_size, -1)
    lowrank = second[:, : row_count * rank_dim].reshape(seg_group, rank_dim, seg_len)
    piece = rank_dim * key_shard
    low_end = row_count * rank_dim
    seg_up = second[:, low_end : low_end + piece].astype(f32)
    seg_up = seg_up + second[:, low_end + piece :].astype(f32)
    seg_up = seg_up.reshape(seg_group, rank_dim, key_shard)
    seg_down = 2.0 * jnp.einsum("srj,sjd->srd", lowrank, input_seg, preferred_element_type=f32)
    seg_grad = jnp.concatenate([seg_down, seg_up], axis=2)
    onehot = (slot_ids[:, None] == seg_slot[None, :]).astype(bf16)
    grad_round = lax.reduce_precision(seg_grad, exponent_bits=8, mantissa_bits=7)
    grad_high = grad_round.astype(bf16)
    grad_low = (seg_grad - grad_round).astype(bf16)
    flat_high = grad_high.reshape(seg_group, -1)
    flat_low = grad_low.reshape(seg_group, -1)
    part = jnp.dot(onehot, flat_high, preferred_element_type=f32)
    part = part + jnp.dot(onehot, flat_low, preferred_element_type=f32)
    part = part.astype(bf16).reshape(group_count, per_owner, -1)
    gathered = lax.all_to_all(part, "dp", 0, 0, tiled=True)
    frozen = lax.dot_general(
        whole_raw, key_weight, (((1,), (1,)), ((), ())), preferred_element_type=f32
    )
    frozen = jnp.where(jnp.repeat(seg_live, seg_len)[:, None], frozen, jnp.zeros_like(frozen))
    extra = jnp.einsum("srj,srd->sjd", lowrank, down_seg, preferred_element_type=f32)
    input_grad = (frozen + 2.0 * extra.reshape(tok_group, width_shard)).astype(bf16)
    gathered, input_grad = lax.optimization_barrier((gathered, input_grad))
    total = jnp.sum(gathered.astype(f32), axis=0).reshape(per_owner, rank_dim, -1)
    down_grad = total[:, :, :width_shard].astype(bf16)
    up_grad = total[:, :, width_shard:].astype(bf16)
    return (input_grad, down_grad, up_grad)


def solution(mesh):
    in_specs = (
        P("dp", "tensor"),
        P(("dp", "tensor"), None),
        P("tensor", None),
        P("dp", None, "tensor"),
        P("dp", None, "tensor"),
        P(),
        P(),
        P("dp"),
    )
    out_specs = (P("dp", "tensor"), P("dp", None, "tensor"), P("dp", None, "tensor"))
    return jax.shard_map(
        on_device, mesh=mesh, in_specs=in_specs, out_specs=out_specs, check_vma=False
    )
```

profile of v0, /device:TPU:1, one launch (start us, length us, event | category | flops | bytes accessed | tf_op | source)
XLA Modules:
  0.0 147.1 jit_solution(13841824733136216324)
XLA Ops:
  7.2 0.0 copy-start
  7.2 0.0 copy-start.5
  7.2 0.0 copy-start.6
  7.2 0.0 all-gather.2.cloned.1.call-start
  7.2 0.7 all-gather.2.cloned.1.call-update
  7.9 0.9 pad_maximum_fusion.2
  8.8 0.1 broadcast_in_dim.54
  9.0 1.1 broadcast_in_dim.55
  10.0 10.4 %all-to-all-start = ((bf16[16,8,4608]{2,1,0:T(8,128)(2,1)}), bf16[16,8,4608]{2,1,0:T(8,128)(2,1)S(1)}, u32[]{:S(2)}, u32[]{:S(2)}) async-start(bf16[16,8,4608]{2,1,0:T(8,128)(2,1)} %broadcast_in_dim.55), calls=%async_computation | async-start | bytes 2359296 | tf_op jit(solution)/shard_map/all_to_all | solution.py:42
  20.4 0.0 copy-done.5
  20.4 0.0 copy-done.6
  20.4 0.2 select_reduce_fusion
  20.7 0.1 dynamic_slice.3
  20.7 30.3 %all-to-all-done = bf16[16,8,4608]{2,1,0:T(8,128)(2,1)S(1)} async-done(((bf16[16,8,4608]{2,1,0:T(8,128)(2,1)}), bf16[16,8,4608]{2,1,0:T(8,128)(2,1)S(1)}, u32[]{:S(2)}, u32[]{:S(2)}) %all-to-all-start) | async-done | bytes 1179680 | tf_op jit(solution)/shard_map/all_to_all | solution.py:42
  51.0 1.1 convolution_convert_fusion
  52.1 1.5 %reshape.65 = bf16[32,16,288]{2,1,0:T(8,128)(2,1)S(1)} reshape(bf16[32,4608]{1,0:T(8,128)(2,1)} %convolution_convert_fusion) | data formatting | bytes 589824 | tf_op jit(solution)/shard_map/reshape | solution.py:45
  53.6 0.0 copy-start.1
  53.6 0.0 copy-done
  53.7 0.6 fusion.10
  54.3 0.0 copy-start.4
  54.3 0.1 pad_maximum_fusion.1
  54.4 1.4 all_to_all.20
  55.8 0.0 copy-done.1
  55.8 11.1 %all-to-all-start.1 = ((f32[32,1,2560]{2,1,0:T(1,128)}), f32[32,1,2560]{2,1,0:T(1,128)S(1)}, u32[]{:S(2)}, u32[]{:S(2)}) async-start(f32[32,1,2560]{2,1,0:T(1,128)} %all_to_all.20), calls=%async_computation.1 | async-start | bytes 655360 | tf_op jit(solution)/shard_map/all_to_all | solution.py:51
  67.5 13.1 %all-to-all-done.1 = f32[32,1,2560]{2,1,0:T(1,128)S(1)} async-done(((f32[32,1,2560]{2,1,0:T(1,128)}), f32[32,1,2560]{2,1,0:T(1,128)S(1)}, u32[]{:S(2)}, u32[]{:S(2)}) %all-to-all-start.1) | async-done | bytes 327712 | tf_op jit(solution)/shard_map/all_to_all | solution.py:51
  80.6 0.8 reduce.1
  81.4 0.3 reshape.67
  81.7 0.0 copy-done.4
  81.7 0.2 convolution_multiply_fusion.2
  81.9 0.1 reshape.68
  82.0 0.2 copy.25
  82.2 0.1 reshape.69
  82.4 0.2 convert_element_type.55
  82.6 0.2 fusion.5
  82.8 16.6 %all_to_all.25 = bf16[32,24,128]{2,1,0:T(8,128)(2,1)S(1)} all-to-all(bf16[32,24,128]{2,1,0:T(8,128)(2,1)S(1)} %bitcast.45), channel_id=1, replica_groups=mesh['dp'=16,'tensor'=32] {'tensor'}, dimensions={0} | all-to-all | bytes 393216 | tf_op jit(solution)/shard_map/all_to_all | solution.py:73
  99.5 0.0 copy-start.2
  99.6 0.1 reshape.73
  99.7 0.4 convolution_multiply_fusion.1
  100.1 0.1 copy-done.2
  100.2 0.1 pad_maximum_fusion
  100.2 0.3 concatenate.18
  100.6 0.4 fusion.8
  101.0 0.0 copy-start.3
  101.0 1.6 %fusion.1 = bf16[16,8,4608]{2,1,0:T(8,128)(2,1)} fusion(f32[128,4608]{1,0:T(8,128)S(1)} %fusion.8, f32[32,4608]{1,0:T(8,128)S(1)} %concatenate.18, s32[32]{0:T(128)S(1)} %dynamic_slice.3), kind=kOutput, calls=%fused_computation.2 | convolution fusion | flops 39374848 | bytes 4128896 | tf_op jit(solution)/shard_map/dot_general | solution.py:89
  102.6 5.5 %all-to-all-start.3 = ((bf16[16,8,4608]{2,1,0:T(8,128)(2,1)}), bf16[16,8,4608]{2,1,0:T(8,128)(2,1)S(1)}, u32[]{:S(2)}, u32[]{:S(2)}) async-start(bf16[16,8,4608]{2,1,0:T(8,128)(2,1)} %fusion.1), calls=%async_computation.3 | async-start | bytes 2359296 | tf_op jit(solution)/shard_map/all_to_all | solution.py:91
  108.1 0.1 broadcast_bitcast_fusion
  108.2 0.0 copy-done.3
  108.2 3.7 %convolution_multiply_fusion = f32[32,128,256]{2,1,0:T(8,128)} fusion(bf16[32,16,128]{2,1,0:T(8,128)(2,1)S(1)} %bitcast.41, bf16[32,16,288]{2,1,0:T(8,128)(2,1)} %copy-done.1), kind=kOutput, calls=%fused_computation.7 | convolution fusion | flops 34603008 | bytes 4587520 | tf_op jit(solution)/shard_map/srj,srd->sjd/dot_general | solution.py:96
  111.8 13.0 %all-gather.2.cloned.1.call-done = bf16[4096,1024]{1,0:T(8,128)(2,1)} async-done(((bf16[128,1024]{1,0:T(8,128)(2,1)}), bf16[4096,1024]{1,0:T(8,128)(2,1)}) %all-gather.2.cloned.1.call-update) | async-done | bytes 8388624 | tf_op jit(solution)/shard_map/all_gather | solution.py:34
  124.9 7.1 %fusion.3 = bf16[4096,256]{1,0:T(8,128)(2,1)} fusion(f32[4096,256]{1,0:T(8,128)} %bitcast.39, bf16[4096,1024]{1,0:T(8,128)(2,1)} %all-gather.2.cloned.1.call-done, bf16[256,1024]{1,0:T(8,128)(2,1)} %param.10, pred[4096]{0:T(1024)(128)(4,1)S(1)} %broadcast_bitcast_fusion), kind=kOutput, calls=%fused_computation.6 | convolution fusion | flops 2150629376 | bytes 15208448 | tf_op jit(solution)/shard_map/dot_general | solution.py:92
  131.9 6.7 %all-to-all-done.3 = bf16[16,8,4608]{2,1,0:T(8,128)(2,1)S(1)} async-done(((bf16[16,8,4608]{2,1,0:T(8,128)(2,1)}), bf16[16,8,4608]{2,1,0:T(8,128)(2,1)S(1)}, u32[]{:S(2)}, u32[]{:S(2)}) %all-to-all-start.3) | async-done | bytes 1179680 | tf_op jit(solution)/shard_map/all_to_all | solution.py:91
  138.7 0.2 reduce
  138.8 0.2 reshape.76
  139.0 0.6 slice.46
  139.7 0.6 slice.47
  (13 shorter events, 0.3 us)
Async XLA Ops:
  7.2 46.5 %copy-start = (bf16[4096,256]{1,0:T(8,128)(2,1)S(1)}, bf16[4096,256]{1,0:T(8,128)(2,1)}, u32[]{:S(2)}) copy-start(bf16[4096,256]{1,0:T(8,128)(2,1)} %param.8) | copy-start | bytes 6291460
  7.2 13.2 %copy-start.5 = (s32[512]{0:T(512)S(1)}, s32[512]{0:T(512)}, u32[]{:S(2)}) copy-start(s32[512]{0:T(512)} %param.13) | copy-start | bytes 6148
  7.2 13.2 %copy-start.6 = (s32[128]{0:T(128)S(1)}, s32[128]{0:T(128)}, u32[]{:S(2)}) copy-start(s32[128]{0:T(128)} %param.14) | copy-start | bytes 1540
  7.2 117.7 %all-gather.2.cloned.1.call-start = ((), (), s32[]{:S(2)}) async-start(), calls=%async_computation.4 | async-start | bytes 8650752 | tf_op jit(solution)/shard_map/all_gather | solution.py:34
  10.0 41.0 %all-to-all-start = ((bf16[16,8,4608]{2,1,0:T(8,128)(2,1)}), bf16[16,8,4608]{2,1,0:T(8,128)(2,1)S(1)}, u32[]{:S(2)}, u32[]{:S(2)}) async-start(bf16[16,8,4608]{2,1,0:T(8,128)(2,1)} %broadcast_in_dim.55), calls=%async_computation | async-start | bytes 2359296 | tf_op jit(solution)/shard_map/all_to_all | solution.py:42
  53.6 2.2 %copy-start.1 = (bf16[32,16,288]{2,1,0:T(8,128)(2,1)}, bf16[32,16,288]{2,1,0:T(8,128)(2,1)S(1)}, u32[]{:S(2)}) copy-start(bf16[32,16,288]{2,1,0:T(8,128)(2,1)S(1)} %reshape.65) | copy-start | bytes 884740
  54.3 27.4 %copy-start.4 = (bf16[128,1024]{1,0:T(8,128)(2,1)S(1)}, bf16[128,1024]{1,0:T(8,128)(2,1)}, u32[]{:S(2)}) copy-start(bf16[128,1024]{1,0:T(8,128)(2,1)} %param.9) | copy-start | bytes 786436
  55.8 24.9 %all-to-all-start.1 = ((f32[32,1,2560]{2,1,0:T(1,128)}), f32[32,1,2560]{2,1,0:T(1,128)S(1)}, u32[]{:S(2)}, u32[]{:S(2)}) async-start(f32[32,1,2560]{2,1,0:T(1,128)} %all_to_all.20), calls=%async_computation.1 | async-start | bytes 655360 | tf_op jit(solution)/shard_map/all_to_all | solution.py:51
  99.5 0.6 copy-start.2
  101.0 7.1 %copy-start.3 = (bf16[4,8,16,128]{3,2,1,0:T(8,128)(2,1)S(1)}, bf16[4,8,16,128]{3,2,1,0:T(8,128)(2,1)}, u32[]{:S(2)}) copy-start(bf16[4,8,16,128]{3,2,1,0:T(8,128)(2,1)} %copy-done.2) | copy-start | bytes 393220
  102.6 36.1 %all-to-all-start.3 = ((bf16[16,8,4608]{2,1,0:T(8,128)(2,1)}), bf16[16,8,4608]{2,1,0:T(8,128)(2,1)S(1)}, u32[]{:S(2)}, u32[]{:S(2)}) async-start(bf16[16,8,4608]{2,1,0:T(8,128)(2,1)} %fusion.1), calls=%async_computation.3 | async-start | bytes 2359296 | tf_op jit(solution)/shard_map/all_to_all | solution.py:91
Sparse Core Ops, SparseCore 0:
  11.2 113.6 all-gather.1
where the time goes:
time: 148 us; the launch traced here: 147 us
  waiting for transfers between devices  63.8 us (43%)
  starting transfers between devices  27 us (18%)
  blocking collectives  16.6 us (11%)
  matrix products  15.2 us (10%)
  between operations  14.9 us (10%)
  local copies, waits for them, and re-layouts  7.34 us (5%)
  other arithmetic  2.28 us (2%)
    all_to_all x1, waiting for transfers between devices, on_device(): lax.all_to_all(spread, 'dp', 0, 0, tiled=True).reshape(adapters, -1)  30.3 us
    all_to_all x1, blocking collectives, on_device(): lax.all_to_all(second, 'tensor', 0, 0, tiled=True).reshape(tensor_size, -1)  16.6 us
    all_to_all x1, waiting for transfers between devices, on_device(): first = lax.all_to_all(first, 'tensor', 0, 0, tiled=True)  13.1 us
    all_gather x1, waiting for transfers between devices, on_device(): whole_raw = lax.all_gather(output_grad, 'tensor', axis=0, tiled=True)  13 us
    all_to_all x1, starting transfers between devices, on_device(): first = lax.all_to_all(first, 'tensor', 0, 0, tiled=True)  11.1 us
    all_to_all x1, starting transfers between devices, on_device(): lax.all_to_all(spread, 'dp', 0, 0, tiled=True).reshape(adapters, -1)  10.4 us
    dot_general x1, matrix products, on_device(): lax.dot_general(whole_raw, key_weight, (((1,), (1,)), ((), ())), preferre...  7.09 us
    all_to_all x1, waiting for transfers between devices, on_device(): gathered = lax.all_to_all(part, 'dp', 0, 0, tiled=True)  6.74 us
  transfers between devices with their start and end apart: 4, of which 4 were waited for; matrix products, arithmetic and copies ran while one was open for 15% of the time, Pallas kernels for 0%

commit v1 on v0

--- a/solution.py
+++ b/solution.py
@@ -31,7 +31,8 @@
     seg_len = tok_group // seg_group
     f32 = jnp.float32
     bf16 = jnp.bfloat16
-    whole_raw = lax.all_gather(output_grad, "tensor", axis=0, tiled=True)
+    repeated = jnp.stack([output_grad] * lax.axis_size("tensor"))
+    whole_raw = jnp.concatenate(lax.all_to_all(repeated, "tensor", 0, 0), axis=0)
     slot_ids = jnp.arange(adapters, dtype=jnp.int32)
     lookup = segment_adapter[:, None] == slot_ids[None, :]
     every_slot = jnp.sum(jnp.where(lookup, adapter_slot[None, :], 0), axis=1)

time: 148 us -> 327 us (2.21)
  waiting for transfers between devices: 63.8 us -> 253 us
  between operations: 14.9 us -> 1.57 us
  starting transfers between devices: 27 us -> 31.4 us
  local copies, waits for them, and re-layouts: 7.34 us -> 11.6 us
    all_to_all x0 -> x1, waiting for transfers between devices: none -> 186 us  [on_device(): lax.all_to_all(repeated, 'tensor', 0, 0)]
    all_to_all x1, waiting for transfers between devices: 6.74 us -> 22.8 us  [on_device(): gathered = lax.all_to_all(part, 'dp', 0, 0, tiled=True)]
    all_gather x1 -> x0, waiting for transfers between devices: 13 us -> none  [on_device(): whole_raw = lax.all_gather(output_grad, 'tensor', axis=0, tiled=True)]
    all_to_all x0 -> x1, starting transfers between devices: none -> 4.97 us  [on_device(): lax.all_to_all(repeated, 'tensor', 0, 0)]
    another operation x1 -> x2, local copies, waits for them, and re-layouts: 0.17 us -> 4.46 us  [the longest x1 4.29 us: on_device(): repeated = jnp.stack([output_grad] * lax.axis_size('tensor'))]
  transfers between devices with their start and end apart: 4 -> 4, of which waited for: 4 -> 4; matrix products, arithmetic and copies ran while one was open for 15% -> 3% of each run, Pallas kernels for 0% -> 0%
where the time goes in v1:
time: 327 us; the launch traced here: 326 us
  waiting for transfers between devices  253 us (77%)
  starting transfers between devices  31.4 us (10%)
  blocking collectives  14.6 us (4%)
  matrix products  12 us (4%)
  local copies, waits for them, and re-layouts  11.6 us (4%)
    all_to_all x1, waiting for transfers between devices, on_device(): lax.all_to_all(repeated, 'tensor', 0, 0)  186 us
    all_to_all x1, waiting for transfers between devices, on_device(): lax.all_to_all(spread, 'dp', 0, 0, tiled=True).reshape(adapters, -1)  30.3 us
    all_to_all x1, waiting for transfers between devices, on_device(): gathered = lax.all_to_all(part, 'dp', 0, 0, tiled=True)  22.8 us
    all_to_all x1, blocking collectives, on_device(): lax.all_to_all(second, 'tensor', 0, 0, tiled=True).reshape(tensor_size, -1)  14.6 us
    all_to_all x1, waiting for transfers between devices, on_device(): first = lax.all_to_all(first, 'tensor', 0, 0, tiled=True)  13.1 us
    all_to_all x1, starting transfers between devices, on_device(): first = lax.all_to_all(first, 'tensor', 0, 0, tiled=True)  11.1 us
    all_to_all x1, starting transfers between devices, on_device(): lax.all_to_all(spread, 'dp', 0, 0, tiled=True).reshape(adapters, -1)  10.4 us
  transfers between devices with their start and end apart: 4, of which 4 were waited for; matrix products, arithmetic and copies ran while one was open for 3% of the time, Pallas kernels for 0%

profile of v1, /device:TPU:1, one launch (start us, length us, event | category | flops | bytes accessed | tf_op | source)
XLA Modules:
  0.0 326.1 jit_solution(9230412032509231447)
XLA Ops:
  0.6 0.0 copy-start
  0.6 0.0 copy-start.5
  0.7 0.0 copy-start.6
  0.7 1.0 pad_maximum_fusion.2
  1.7 0.1 broadcast_in_dim.54
  1.8 1.1 broadcast_in_dim.55
  2.9 10.4 %all-to-all-start = ((bf16[16,8,4608]{2,1,0:T(8,128)(2,1)}), bf16[16,8,4608]{2,1,0:T(8,128)(2,1)S(1)}, u32[]{:S(2)}, u32[]{:S(2)}) async-start(bf16[16,8,4608]{2,1,0:T(8,128)(2,1)} %broadcast_in_dim.55), calls=%async_computation | async-start | bytes 2359296 | tf_op jit(solution)/shard_map/all_to_all | solution.py:43
  13.3 0.0 copy-done.5
  13.3 0.0 copy-done.6
  13.3 0.2 select_reduce_fusion
  13.5 0.1 dynamic_slice.3
  13.6 30.3 %all-to-all-done = bf16[16,8,4608]{2,1,0:T(8,128)(2,1)S(1)} async-done(((bf16[16,8,4608]{2,1,0:T(8,128)(2,1)}), bf16[16,8,4608]{2,1,0:T(8,128)(2,1)S(1)}, u32[]{:S(2)}, u32[]{:S(2)}) %all-to-all-start) | async-done | bytes 1179680 | tf_op jit(solution)/shard_map/all_to_all | solution.py:43
  43.9 1.1 convolution_convert_fusion
  44.9 1.5 reshape.70
  46.5 0.0 copy-start.1
  46.5 0.0 copy-done
  46.5 0.6 fusion.10
  47.2 0.0 copy-start.4
  47.2 0.1 pad_maximum_fusion.1
  47.2 1.4 all_to_all.24
  48.6 0.0 copy-done.1
  48.6 11.1 %all-to-all-start.1 = ((f32[32,1,2560]{2,1,0:T(1,128)}), f32[32,1,2560]{2,1,0:T(1,128)S(1)}, u32[]{:S(2)}, u32[]{:S(2)}) async-start(f32[32,1,2560]{2,1,0:T(1,128)} %all_to_all.24), calls=%async_computation.1 | async-start | bytes 655360 | tf_op jit(solution)/shard_map/all_to_all | solution.py:52
  60.4 13.1 %all-to-all-done.1 = f32[32,1,2560]{2,1,0:T(1,128)S(1)} async-done(((f32[32,1,2560]{2,1,0:T(1,128)}), f32[32,1,2560]{2,1,0:T(1,128)S(1)}, u32[]{:S(2)}, u32[]{:S(2)}) %all-to-all-start.1) | async-done | bytes 327712 | tf_op jit(solution)/shard_map/all_to_all | solution.py:52
  73.5 0.8 reduce.1
  74.2 0.3 reshape.72
  74.6 0.0 copy-done.4
  74.6 0.2 convolution_multiply_fusion.2
  74.8 0.1 reshape.73
  74.9 0.2 copy.25
  75.0 0.1 reshape.74
  75.2 0.2 convert_element_type.55
  75.4 0.2 fusion.5
  75.6 0.1 maximum_bitcast_fusion
  75.7 14.6 %all_to_all.30 = bf16[32,24,128]{2,1,0:T(8,128)(2,1)S(1)} all-to-all(bf16[32,24,128]{2,1,0:T(8,128)(2,1)S(1)} %bitcast.47), channel_id=1, replica_groups=mesh['dp'=16,'tensor'=32] {'tensor'}, dimensions={0} | all-to-all | bytes 393216 | tf_op jit(solution)/shard_map/all_to_all | solution.py:74
  90.2 4.3 %stack.2 = bf16[32,128,1024]{2,1,0:T(8,128)(2,1)} broadcast(bf16[128,1024]{1,0:T(8,128)(2,1)S(1)} %copy-done.4), dimensions={1,2} | broadcast | bytes 8650752 | tf_op jit(solution)/shard_map/stack | solution.py:34
  94.5 5.0 %all-to-all-start.4 = ((bf16[32,128,1024]{2,1,0:T(8,128)(2,1)}), bf16[32,128,1024]{2,1,0:T(8,128)(2,1)}, u32[]{:S(2)}, u32[]{:S(2)}) async-start(bf16[32,128,1024]{2,1,0:T(8,128)(2,1)} %stack.2), calls=%async_computation.4 | async-start | bytes 16777216 | tf_op jit(solution)/shard_map/all_to_all | solution.py:35
  99.6 0.0 copy-start.2
  99.6 0.1 reshape.78
  99.7 0.4 convolution_multiply_fusion.1
  100.1 0.1 copy-done.2
  100.2 0.1 pad_maximum_fusion
  100.3 0.3 concatenate.18
  100.6 0.4 fusion.8
  101.1 0.0 copy-start.3
  101.1 1.5 fusion.1
  102.6 186.4 %all-to-all-done.4 = bf16[32,128,1024]{2,1,0:T(8,128)(2,1)} async-done(((bf16[32,128,1024]{2,1,0:T(8,128)(2,1)}), bf16[32,128,1024]{2,1,0:T(8,128)(2,1)}, u32[]{:S(2)}, u32[]{:S(2)}) %all-to-all-start.4) | async-done | bytes 8388640 | tf_op jit(solution)/shard_map/all_to_all | solution.py:35
  288.9 5.0 %all-to-all-start.3 = ((bf16[16,8,4608]{2,1,0:T(8,128)(2,1)}), bf16[16,8,4608]{2,1,0:T(8,128)(2,1)S(1)}, u32[]{:S(2)}, u32[]{:S(2)}) async-start(bf16[16,8,4608]{2,1,0:T(8,128)(2,1)} %fusion.1), calls=%async_computation.3 | async-start | bytes 2359296 | tf_op jit(solution)/shard_map/all_to_all | solution.py:92
  293.9 0.0 copy-start.7
  293.9 0.1 broadcast_bitcast_fusion
  294.0 0.0 copy-done.3
  294.0 1.8 convolution_multiply_fusion
  295.8 0.0 copy-done.7
  295.8 5.9 %fusion.3 = bf16[4096,256]{1,0:T(8,128)(2,1)} fusion(f32[4096,256]{1,0:T(8,128)S(1)} %bitcast.40, bf16[4096,1024]{1,0:T(8,128)(2,1)} %bitcast.8, bf16[256,1024]{1,0:T(8,128)(2,1)S(1)} %copy-done.7, pred[4096]{0:T(1024)(128)(4,1)S(1)} %broadcast_bitcast_fusion), kind=kOutput, calls=%fused_computation.6 | convolution fusion | flops 2150629376 | bytes 15208448 | tf_op jit(solution)/shard_map/dot_general | solution.py:93
  301.7 22.8 %all-to-all-done.3 = bf16[16,8,4608]{2,1,0:T(8,128)(2,1)S(1)} async-done(((bf16[16,8,4608]{2,1,0:T(8,128)(2,1)}), bf16[16,8,4608]{2,1,0:T(8,128)(2,1)S(1)}, u32[]{:S(2)}, u32[]{:S(2)}) %all-to-all-start.3) | async-done | bytes 1179680 | tf_op jit(solution)/shard_map/all_to_all | solution.py:92
  324.5 0.2 reduce
  324.7 0.2 reshape.82
  324.9 0.6 slice.46
  325.5 0.6 slice.47
  (12 shorter events, 0.2 us)
Async XLA Ops:
  0.6 45.9 %copy-start = (bf16[4096,256]{1,0:T(8,128)(2,1)S(1)}, bf16[4096,256]{1,0:T(8,128)(2,1)}, u32[]{:S(2)}) copy-start(bf16[4096,256]{1,0:T(8,128)(2,1)} %param.8) | copy-start | bytes 6291460
  0.6 12.6 %copy-start.5 = (s32[512]{0:T(512)S(1)}, s32[512]{0:T(512)}, u32[]{:S(2)}) copy-start(s32[512]{0:T(512)} %param.13) | copy-start | bytes 6148
  0.7 12.6 %copy-start.6 = (s32[128]{0:T(128)S(1)}, s32[128]{0:T(128)}, u32[]{:S(2)}) copy-start(s32[128]{0:T(128)} %param.14) | copy-start | bytes 1540
  2.9 41.0 %all-to-all-start = ((bf16[16,8,4608]{2,1,0:T(8,128)(2,1)}), bf16[16,8,4608]{2,1,0:T(8,128)(2,1)S(1)}, u32[]{:S(2)}, u32[]{:S(2)}) async-start(bf16[16,8,4608]{2,1,0:T(8,128)(2,1)} %broadcast_in_dim.55), calls=%async_computation | async-start | bytes 2359296 | tf_op jit(solution)/shard_map/all_to_all | solution.py:43
  46.5 2.1 copy-start.1
  47.2 27.4 %copy-start.4 = (bf16[128,1024]{1,0:T(8,128)(2,1)S(1)}, bf16[128,1024]{1,0:T(8,128)(2,1)}, u32[]{:S(2)}) copy-start(bf16[128,1024]{1,0:T(8,128)(2,1)} %param.9) | copy-start | bytes 786436
  48.6 24.9 %all-to-all-start.1 = ((f32[32,1,2560]{2,1,0:T(1,128)}), f32[32,1,2560]{2,1,0:T(1,128)S(1)}, u32[]{:S(2)}, u32[]{:S(2)}) async-start(f32[32,1,2560]{2,1,0:T(1,128)} %all_to_all.24), calls=%async_computation.1 | async-start | bytes 655360 | tf_op jit(solution)/shard_map/all_to_all | solution.py:52
  94.5 194.4 %all-to-all-start.4 = ((bf16[32,128,1024]{2,1,0:T(8,128)(2,1)}), bf16[32,128,1024]{2,1,0:T(8,128)(2,1)}, u32[]{:S(2)}, u32[]{:S(2)}) async-start(bf16[32,128,1024]{2,1,0:T(8,128)(2,1)} %stack.2), calls=%async_computation.4 | async-start | bytes 16777216 | tf_op jit(solution)/shard_map/all_to_all | solution.py:35
  99.6 0.6 copy-start.2
  101.1 192.9 %copy-start.3 = (bf16[4,8,16,128]{3,2,1,0:T(8,128)(2,1)S(1)}, bf16[4,8,16,128]{3,2,1,0:T(8,128)(2,1)}, u32[]{:S(2)}) copy-start(bf16[4,8,16,128]{3,2,1,0:T(8,128)(2,1)} %copy-done.2) | copy-start | bytes 393220
  288.9 35.6 %all-to-all-start.3 = ((bf16[16,8,4608]{2,1,0:T(8,128)(2,1)}), bf16[16,8,4608]{2,1,0:T(8,128)(2,1)S(1)}, u32[]{:S(2)}, u32[]{:S(2)}) async-start(bf16[16,8,4608]{2,1,0:T(8,128)(2,1)} %fusion.1), calls=%async_computation.3 | async-start | bytes 2359296 | tf_op jit(solution)/shard_map/all_to_all | solution.py:92
  293.9 1.9 copy-start.7
